TPU v7x, 256 devices: a whole 4x4x8 slice. The times are simulated.
256 devices in a mesh: seq: 16 (over y, x), fsdp: 16 (over z, core).
Axes of the slice: x: 4, y: 4, z: 8, core: 2. Of those that a mesh axis runs over, the one named last changes fastest.
Arguments:
- byte_rows: bfloat16 [16, 16384, 512], P('fsdp', 'seq'), may hold values from -6 to 6
- cotangent: bfloat16 [16, 16384, 512], P('fsdp', 'seq'), may hold values from -6 to 6
- doc_ids: int32 [16, 16384], P('fsdp', 'seq'), may hold values from 0 to 31, never falling along the last dimension, each value on 1 to 2048 neighbouring positions
- conv_weight: bfloat16 [8, 32, 16, 16], replicated, may hold values from -0.5 to 0.5
- norm_gain: float32 [512], replicated, may hold values from 0.5 to 1.5
- proj_weight: bfloat16 [4096, 512], P('fsdp'), may hold values from -0.25 to 0.25
- round_seed: int32 [1], replicated, may hold values from 0 to 1073741823
- step_count: int32 [1], replicated, may hold values from 0 to 999999
Outputs:
- grad_bytes: float32 [16, 16384, 512], P('fsdp', 'seq')
- grad_proj: float32 [4096, 512], P('fsdp')
- grad_conv: float32 [8, 32, 16, 16], replicated
- grad_gain: float32 [512], replicated
Inputs may be any that keep to these rules, and one draw needn't show every extreme that they name: `doc_ids`: along each sequence the document numbers never fall; no document covers more than 2048 bytes, and one covers exactly 2048.
All inputs are finite; a program needn't handle non-finite values.
Results may differ from a plain program's by a relative error of at most 0.0046.
Values may be sent and summed in bfloat16 or wider, within the bound.
No kernel may reach another device: no remote copies, remote signals or barrier semaphores. Data moves between devices by JAX's collectives and lax.ppermute only.
A program may use at most 128 MiB of HBM per device.

v0:
```python
import math
import jax
import jax.numpy as jnp
from jax import lax
from jax.sharding import PartitionSpec as P

GROUPS = 32
KERNEL = 8
STRIDE = 4
CG = 16
GELU_A = 0.7978845608028654
GELU_B = 0.044715
QUANT = 0.25


def shifted(value, axis, steps):
    count = lax.axis_size(axis)
    initial, last = (max(0, -steps), min(count, count - steps))
    return lax.ppermute(value, axis, [(source, source + steps) for source in range(initial, last)])


def gelu_grad(values):
    tangent = jnp.tanh(GELU_A * (values + GELU_B * values * values * values))
    return 0.5 * (1.0 + tangent) + 0.5 * values * (1.0 - tangent * tangent) * GELU_A * (
        1.0 + 3.0 * GELU_B * values * values
    )


def mix_bits(flat_index, seed_value, step_value):
    hashed = (
        flat_index * jnp.int32(-1640531535)
        + seed_value * jnp.int32(-2048144777)
        + step_value * jnp.int32(-1028477379)
    )
    hashed = hashed ^ lax.shift_right_logical(hashed, jnp.int32(16))
    hashed = hashed * jnp.int32(2146121005)
    hashed = hashed ^ lax.shift_right_logical(hashed, jnp.int32(15))
    hashed = hashed * jnp.int32(-2073254261)
    hashed = hashed ^ lax.shift_right_logical(hashed, jnp.int32(16))
    return lax.shift_right_logical(hashed, jnp.int32(8)).astype(jnp.float32) / 16777216.0


def split_bf16(value):
    high = value.astype(jnp.bfloat16)
    low = (value - high.astype(jnp.float32)).astype(jnp.bfloat16)
    return (high, low)


def dot_f32(lhs, rhs, dims):
    return lax.dot_general(lhs, rhs, (dims, ((), ())), preferred_element_type=jnp.float32)


def per_device(
    byte_rows, cotangent, doc_ids, conv_weight, norm_gain, proj_weight, round_seed, step_count
):
    byte_block = byte_rows[0]
    upstream = cotangent[0]
    doc_block = doc_ids[0]
    length = byte_block.shape[0]
    row_width = byte_block.shape[1]
    patches = length // STRIDE
    half = STRIDE * row_width
    panel_rows = proj_weight.shape[0]
    next_bytes, next_up, next_docs = shifted(
        (byte_block[:STRIDE], upstream[:STRIDE], doc_block[:STRIDE]), "seq", -1
    )
    bytes_lo = byte_block.reshape(patches, half)
    bytes_hi = jnp.concatenate([bytes_lo[1:], next_bytes.reshape(1, half)], 0)
    up_lo = upstream.reshape(patches, half)
    up_hi = jnp.concatenate([up_lo[1:], next_up.reshape(1, half)], 0)
    docs_lo = doc_block.reshape(patches, STRIDE)
    docs_hi = jnp.concatenate([docs_lo[1:], next_docs.reshape(1, STRIDE)], 0)
    is_last = lax.axis_index("seq") == lax.axis_size("seq") - 1
    patch_ids = lax.broadcasted_iota(jnp.int32, (patches, STRIDE), 0)
    spilled = is_last & (patch_ids == patches - 1)
    keep_lo = docs_lo == docs_lo[:, :1]
    keep_hi = (docs_hi == docs_lo[:, :1]) & jnp.logical_not(spilled)

    def spread(keep):
        return jnp.broadcast_to(keep[:, :, None], (patches, STRIDE, row_width)).reshape(
            patches, half
        )

    keep_lo_f = spread(keep_lo.astype(jnp.float32))
    keep_hi_f = spread(keep_hi.astype(jnp.float32))
    win_lo = bytes_lo * keep_lo_f.astype(jnp.bfloat16)
    win_hi = bytes_hi * keep_hi_f.astype(jnp.bfloat16)
    group_eye = jnp.eye(GROUPS, dtype=jnp.bfloat16)
    dense_weight = (conv_weight[:, :, :, None, :] * group_eye[None, :, None, :, None]).reshape(
        KERNEL, row_width, row_width
    )
    weight_lo = dense_weight[:STRIDE].reshape(half, row_width)
    weight_hi = dense_weight[STRIDE:].reshape(half, row_width)
    hidden = dot_f32(win_lo, weight_lo, ((1,), (0,))) + dot_f32(win_hi, weight_hi, ((1,), (0,)))
    factor = lax.rsqrt(jnp.mean(hidden * hidden, axis=-1, keepdims=True) + 1e-06)
    normed = (hidden * factor * norm_gain).astype(jnp.bfloat16)
    full_proj = lax.all_gather(proj_weight, "fsdp", axis=0, tiled=True)
    proj_lo = full_proj[:half]
    proj_hi = full_proj[half:]
    pre_lo = dot_f32(normed, proj_lo, ((1,), (1,)))
    pre_hi = dot_f32(normed, proj_hi, ((1,), (1,)))
    grad_pre_lo = (up_lo.astype(jnp.float32) * keep_lo_f * gelu_grad(pre_lo)).astype(jnp.bfloat16)
    grad_pre_hi = (up_hi.astype(jnp.float32) * keep_hi_f * gelu_grad(pre_hi)).astype(jnp.bfloat16)
    proj_part = jnp.concatenate(
        [dot_f32(grad_pre_lo, normed, ((0,), (0,))), dot_f32(grad_pre_hi, normed, ((0,), (0,)))], 0
    )
    panel_part = lax.psum_scatter(proj_part, "fsdp", scatter_dimension=0, tiled=True)
    grad_norm = dot_f32(grad_pre_lo, proj_lo, ((1,), (0,))) + dot_f32(
        grad_pre_hi, proj_hi, ((1,), (0,))
    )
    gain_part = jnp.sum(grad_norm * hidden * factor, axis=0)
    gained = norm_gain * grad_norm
    grad_hidden = factor * gained - hidden * factor * factor * factor * jnp.mean(
        gained * hidden, axis=-1, keepdims=True
    )
    gh_high, gh_low = split_bf16(grad_hidden)

    def window_grad(window):
        full = dot_f32(window, gh_high, ((0,), (0,))) + dot_f32(window, gh_low, ((0,), (0,)))
        blocks = full.reshape(STRIDE, GROUPS, CG, GROUPS, CG)
        mask = jnp.eye(GROUPS, dtype=jnp.float32)[None, :, None, :, None]
        return jnp.sum(blocks * mask, axis=3)

    conv_part = jnp.concatenate([window_grad(win_lo), window_grad(win_hi)], 0)

    def back_taps(weight, keep_f):
        taps = dot_f32(gh_high, weight, ((1,), (1,))) + dot_f32(gh_low, weight, ((1,), (1,)))
        return (taps * keep_f).reshape(length, row_width)

    back_lower = back_taps(weight_lo, keep_lo_f)
    back_upper = back_taps(weight_hi, keep_hi_f)
    incoming = shifted(back_upper[length - STRIDE :], "seq", 1)
    back_rows = back_lower + jnp.concatenate([incoming, back_upper[: length - STRIDE]], 0)
    grad_bytes = (upstream.astype(jnp.float32) + back_rows)[None]
    conv_size = conv_part.size
    small = jnp.concatenate([conv_part.reshape(-1), gain_part]).reshape(-1, row_width)
    small = lax.psum(small, "fsdp")
    joined = lax.psum(jnp.concatenate([panel_part, small], 0), "seq")
    proj_sum = joined[:panel_rows]
    small_sum = joined[panel_rows:].reshape(-1)
    conv_sum = small_sum[:conv_size].reshape(conv_part.shape)
    gain_sum = small_sum[conv_size:]
    total_patches = patches * lax.axis_size("seq") * lax.axis_size("fsdp")
    grad_scale = 1.0 / math.sqrt(total_patches)
    first_panel = lax.axis_index("fsdp") * jnp.int32(panel_rows)
    row_index = first_panel + jnp.arange(panel_rows, dtype=jnp.int32)
    flat_index = (
        row_index[:, None] * jnp.int32(row_width) + jnp.arange(row_width, dtype=jnp.int32)[None, :]
    )
    dither_noise = mix_bits(flat_index, round_seed[0], step_count[0])
    grad_proj = proj_sum * grad_scale + QUANT * (dither_noise - 0.5)
    return (grad_bytes, grad_proj, conv_sum * grad_scale, gain_sum * grad_scale)


def solution(mesh):
    in_specs = (
        P("fsdp", "seq", None),
        P("fsdp", "seq", None),
        P("fsdp", "seq"),
        P(),
        P(),
        P("fsdp", None),
        P(),
        P(),
    )
    out_specs = (P("fsdp", "seq", None), P("fsdp", None), P(), P())
    return jax.shard_map(
        per_device, mesh=mesh, in_specs=in_specs, out_specs=out_specs, check_vma=False
    )
```

profile of v0, /device:TPU:32, one launch (start us, length us, event | category | flops | bytes accessed | tf_op | source)
XLA Modules:
  0.0 527.3 jit_solution(15065183540422117678)
XLA Ops:
  28.2 11.2 %broadcast_multiply_fusion = bf16[8,32,16,32,16]{4,3,2,1,0:T(8,128)(2,1)} fusion(bf16[32,32]{1,0:T(8,128)(2,1)S(1)} %fusion.39, bf16[8,32,16,16]{3,2,1,0:T(8,128)(2,1)S(1)} %copy.23), kind=kLoop, calls=%fused_computation.2 | loop fusion | flops 2097152 | bytes 4327424 | tf_op jit(solution)/shard_map/mul | solution.py:89
  39.4 25.7 %fusion.44 = (bf16[4,32,16,32,16]{4,3,2,1,0:T(8,128)(2,1)}, bf16[4,32,16,32,16]{4,3,2,1,0:T(8,128)(2,1)}) fusion(bf16[8,32,16,32,16]{4,3,2,1,0:T(8,128)(2,1)} %broadcast_multiply_fusion), kind=kLoop, calls=%fused_computation.87 | loop fusion | bytes 8388608 | tf_op jit(solution)/shard_map/slice | solution.py:93
  65.1 28.7 %reshape.252 = bf16[2048,512]{1,0:T(8,128)(2,1)} reshape(bf16[4,32,16,32,16]{4,3,2,1,0:T(8,128)(2,1)} %get-tuple-element.29) | data formatting | bytes 4194304 | tf_op jit(solution)/shard_map/reshape | solution.py:92
  93.8 28.2 %reshape.253 = bf16[2048,512]{1,0:T(8,128)(2,1)S(1)} reshape(bf16[4,32,16,32,16]{4,3,2,1,0:T(8,128)(2,1)} %get-tuple-element.28) | data formatting | bytes 4194304 | tf_op jit(solution)/shard_map/reshape | solution.py:93
  123.6 2.6 fusion.45
  126.9 2.2 copy.32
  134.1 4.3 fusion.15
  138.5 2.9 fusion.49
  145.2 2.7 fusion.48
  152.2 2.8 convolution_add_fusion.1
  155.1 19.8 %reshape.258 = f32[4,32,16,32,16]{4,3,2,1,0:T(8,128)} reshape(f32[2048,512]{1,0:T(8,128)} %convolution_add_fusion.1) | data formatting | bytes 8388608 | tf_op jit(solution)/shard_map/reshape | solution.py:120
  176.6 2.8 convolution_add_fusion
  179.4 19.8 %reshape.260 = f32[4,32,16,32,16]{4,3,2,1,0:T(8,128)} reshape(f32[2048,512]{1,0:T(8,128)} %convolution_add_fusion) | data formatting | bytes 8388608 | tf_op jit(solution)/shard_map/reshape | solution.py:120
  199.2 25.5 %multiply_reduce_fusion.1 = (f32[4,32,16,16]{3,2,1,0:T(8,128)S(1)}, f32[4,32,16,16]{3,2,1,0:T(8,128)}) fusion(f32[4,32,16,32,16]{4,3,2,1,0:T(8,128)} %reshape.258, f32[32,32]{1,0:T(8,128)S(1)} %fusion.38, f32[4,32,16,32,16]{4,3,2,1,0:T(8,128)} %reshape.260), kind=kLoop, calls=%fused_computation.1 | loop fusion | flops 4128768 | bytes 8654848 | tf_op jit(solution)/shard_map/reduce_sum | solution.py:122
  224.7 2.7 pad_maximum_fusion.1
  230.5 7.7 %pad_maximum_fusion = f32[4096,512]{1,0:T(8,128)} fusion(f32[2048,512]{1,0:T(8,128)} %fusion.49, f32[2048,512]{1,0:T(8,128)} %fusion.48), kind=kLoop, calls=%fused_computation.3 | loop fusion | flops 2097152 | bytes 16777216 | tf_op jit(solution)/shard_map/concatenate | solution.py:104
  243.4 5.8 %collective-permute-start.3 = (f32[4,512]{1,0:T(4,128)S(1)}, f32[4,512]{1,0:T(4,128)S(1)}, u32[]{:S(2)}, u32[]{:S(2)}) collective-permute-start(f32[4,512]{1,0:T(4,128)S(1)} %slice.92), channel_id=1, source_target_pairs={{0,16},{16,32},{32,48},{48,64},{64,80},{80,96},{96,112},{112,128},... | collective-permute-start | bytes 24584 | tf_op jit(solution)/shard_map/ppermute | solution.py:19
  249.2 3.7 fusion.46
  252.9 89.3 %all-reduce.3.cloned.1.call-done = f32[129,512]{1,0:T(8,128)} async-done(((f32[129,512]{1,0:T(8,128)}), f32[129,512]{1,0:T(8,128)}) %all-reduce.3.cloned.1.call-update) | async-done | bytes 264208 | tf_op jit(solution)/shard_map/psum | solution.py:137
  342.1 71.0 %reduce-scatter.2.cloned.1.call-done = f32[256,512]{1,0:T(8,128)} async-done(((f32[4096,512]{1,0:T(8,128)}), f32[256,512]{1,0:T(8,128)}) %reduce-scatter.2.cloned.1.call-update) | async-done | bytes 524304 | tf_op jit(solution)/shard_map/reduce_scatter | solution.py:107
  415.3 4.3 fusion.1
  419.6 3.0 reshape.257
  424.5 4.1 fusion.16
  428.6 86.9 %all-reduce.5.cloned.1.call-done = f32[385,512]{1,0:T(8,128)} async-done(((f32[385,512]{1,0:T(8,128)}), f32[385,512]{1,0:T(8,128)}) %all-reduce.5.cloned.1.call-update) | async-done | bytes 788496 | tf_op jit(solution)/shard_map/psum | solution.py:138
  (127 shorter events, 53.7 us)
Async XLA Ops:
  7.2 10.6 %copy-start.5 = (bf16[1,1024,512]{2,1,0:T(8,128)(2,1)S(1)}, bf16[1,1024,512]{2,1,0:T(8,128)(2,1)}, u32[]{:S(2)}) copy-start(bf16[1,1024,512]{2,1,0:T(8,128)(2,1)} %param.9) | copy-start | bytes 3145732
  7.2 126.9 %all-gather.2.cloned.1.call-start = ((), (), s32[]{:S(2)}) async-start(), calls=%async_computation.1 | async-start | bytes 4456448 | tf_op jit(solution)/shard_map/all_gather | solution.py:97
  8.0 118.3 %collective-permute-start.1 = (s32[4]{0:T(128)S(1)}, s32[4]{0:T(128)S(1)}, u32[]{:S(2)}, u32[]{:S(2)}) collective-permute-start(s32[4]{0:T(128)S(1)} %slice_bitcast_fusion.2), channel_id=1, source_target_pairs={{16,0},{32,16},{48,32},{64,48},{80,64},{96,80},{112,96},{128,112},... | collective-permute-start | bytes 56 | tf_op jit(solution)/shard_map/ppermute | solution.py:19
  10.0 120.7 %collective-permute-start = (bf16[4,512]{1,0:T(4,128)(2,1)S(1)}, bf16[4,512]{1,0:T(4,128)(2,1)S(1)}, u32[]{:S(2)}, u32[]{:S(2)}) collective-permute-start(bf16[4,512]{1,0:T(4,128)(2,1)S(1)} %slice_bitcast_fusion.1), channel_id=1, source_target_pairs={{16,0},{32,16},{48,32},{64,48},{80,64},{96,80},{112,96},{128,112},... | collective-permute-start | bytes 12296 | tf_op jit(solution)/shard_map/ppermute | solution.py:19
  11.9 120.2 %collective-permute-start.2 = (bf16[4,512]{1,0:T(4,128)(2,1)S(1)}, bf16[4,512]{1,0:T(4,128)(2,1)S(1)}, u32[]{:S(2)}, u32[]{:S(2)}) collective-permute-start(bf16[4,512]{1,0:T(4,128)(2,1)S(1)} %slice_bitcast_fusion), channel_id=1, source_target_pairs={{16,0},{32,16},{48,32},{64,48},{80,64},{96,80},{112,96},{128,112},... | collective-permute-start | bytes 12296 | tf_op jit(solution)/shard_map/ppermute | solution.py:19
  13.3 328.9 %all-reduce.3.cloned.1.call-start = ((), (), s32[]{:S(2)}) async-start(), calls=%async_computation.3 | async-start | bytes 557056 | tf_op jit(solution)/shard_map/psum | solution.py:137
  19.0 1.6 copy-start.4
  22.0 3.6 copy-start.20
  25.7 1.7 copy-start.19
  93.8 28.2 %copy-start.14 = (bf16[1,1020,512]{2,1,0:T(8,128)(2,1)S(1)}, bf16[1,1020,512]{2,1,0:T(8,128)(2,1)}, u32[]{:S(2)}) copy-start(bf16[1,1020,512]{2,1,0:T(8,128)(2,1)} %slice.86) | copy-start | bytes 3133444
  130.7 3.1 copy-start.2
  132.2 1.6 copy-start.15
  138.4 2.9 copy-start
  138.4 3.4 copy-start.17
  138.5 5.0 copy-start.22
  150.1 2.1 copy-start.10
  230.4 182.7 %reduce-scatter.2.cloned.1.call-start = ((), (), s32[]{:S(2)}) async-start(), calls=%async_computation.2 | async-start | bytes 8912896 | tf_op jit(solution)/shard_map/reduce_scatter | solution.py:107
  238.2 277.3 %all-reduce.5.cloned.1.call-start = ((), (), s32[]{:S(2)}) async-start(), calls=%async_computation.4 | async-start | bytes 1605632 | tf_op jit(solution)/shard_map/psum | solution.py:138
  239.6 1.6 copy-start.3
  243.4 181.1 %collective-permute-start.3 = (f32[4,512]{1,0:T(4,128)S(1)}, f32[4,512]{1,0:T(4,128)S(1)}, u32[]{:S(2)}, u32[]{:S(2)}) collective-permute-start(f32[4,512]{1,0:T(4,128)S(1)} %slice.92), channel_id=1, source_target_pairs={{0,16},{16,32},{32,48},{48,64},{64,80},{80,96},{96,112},{112,128},... | collective-permute-start | bytes 24584 | tf_op jit(solution)/shard_map/ppermute | solution.py:19
  252.9 162.4 %copy-start.1 = (f32[32,8,4,512]{3,1,2,0:T(8,128)S(1)}, f32[32,8,4,512]{3,1,2,0:T(8,128)}, u32[]{:S(2)}) copy-start(f32[32,8,4,512]{3,1,2,0:T(8,128)} %copy.32) | copy-start | bytes 6291460
  419.6 3.0 copy-start.9
  422.6 1.9 copy-start.6
  517.2 1.8 copy-start.18
  (7 other events, 8.0 us)
Sparse Core Ops, SparseCore 0:
  13.4 50.0 all-gather.1
  230.6 111.5 all-reduce.2
  344.9 68.2 reduce-scatter.1
  417.3 98.1 all-reduce.4
where the time goes:
time: 529 us; the launch traced here: 527 us
  waiting for transfers between devices  247 us (47%)
  local copies, waits for them, and re-layouts  161 us (30%)
  other arithmetic  59.2 us (11%)
  matrix products  34.6 us (7%)
  between operations  15.6 us (3%)
  starting transfers between devices  9.79 us (2%)
    psum x1, waiting for transfers between devices, per_device(): small = lax.psum(small, 'fsdp')  89.3 us
    psum x1, waiting for transfers between devices, per_device(): joined = lax.psum(jnp.concatenate([panel_part, small], 0), 'seq')  86.9 us
    reduce_scatter x1, waiting for transfers between devices, per_device(): lax.psum_scatter(proj_part, 'fsdp', scatter_dimension=0, tiled=True)  71 us
    reshape x2, local copies, waits for them, and re-layouts, window_grad(): blocks = full.reshape(STRIDE, GROUPS, CG, GROUPS, CG)  39.7 us
    dot_general x16, matrix products, dot_f32(): lax.dot_general(lhs, rhs, (dims, ((), ())), preferred_element_type=jnp.fl...  34.6 us
    reshape x1, local copies, waits for them, and re-layouts, per_device(): weight_lo = dense_weight[:STRIDE].reshape(half, row_width)  28.7 us
    reshape x1, local copies, waits for them, and re-layouts, per_device(): weight_hi = dense_weight[STRIDE:].reshape(half, row_width)  28.2 us
    slice x1, local copies, waits for them, and re-layouts, per_device(): weight_hi = dense_weight[STRIDE:].reshape(half, row_width)  25.7 us
  transfers between devices with their start and end apart: 8, of which 3 were waited for; matrix products, arithmetic and copies ran while one was open for 28% of the time, Pallas kernels for 0%

commit v1 on v0

--- a/solution.py
+++ b/solution.py
@@ -134,7 +134,7 @@
     grad_bytes = (upstream.astype(jnp.float32) + back_rows)[None]
     conv_size = conv_part.size
     small = jnp.concatenate([conv_part.reshape(-1), gain_part]).reshape(-1, row_width)
-    small = lax.psum(small, "fsdp")
+    small = jnp.sum(lax.all_gather(small, "fsdp"), axis=0)
     joined = lax.psum(jnp.concatenate([panel_part, small], 0), "seq")
     proj_sum = joined[:panel_rows]
     small_sum = joined[panel_rows:].reshape(-1)

time: 529 us -> 462 us (0.87)
  waiting for transfers between devices: 247 us -> 182 us
    psum x1 -> x0, waiting for transfers between devices: 89.3 us -> none  [per_device(): small = lax.psum(small, 'fsdp')]
    all_gather x0 -> x1, waiting for transfers between devices: none -> 29.1 us  [per_device(): small = jnp.sum(lax.all_gather(small, 'fsdp'), axis=0)]
    unnamed x54 -> x66, local copies, waits for them, and re-layouts: 13.2 us -> 12.8 us
  transfers between devices with their start and end apart: 8 -> 8, of which waited for: 3 -> 3; matrix products, arithmetic and copies ran while one was open for 28% -> 33% of each run, Pallas kernels for 0% -> 0%
where the time goes in v1:
time: 462 us; the launch traced here: 461 us
  waiting for transfers between devices  182 us (39%)
  local copies, waits for them, and re-layouts  162 us (35%)
  other arithmetic  60.1 us (13%)
  matrix products  31.3 us (7%)
  between operations  15.7 us (3%)
  starting transfers between devices  9.83 us (2%)
    psum x1, waiting for transfers between devices, per_device(): joined = lax.psum(jnp.concatenate([panel_part, small], 0), 'seq')  86.7 us
    reduce_scatter x1, waiting for transfers between devices, per_device(): lax.psum_scatter(proj_part, 'fsdp', scatter_dimension=0, tiled=True)  65.7 us
    reshape x2, local copies, waits for them, and re-layouts, window_grad(): blocks = full.reshape(STRIDE, GROUPS, CG, GROUPS, CG)  39.6 us
    dot_general x16, matrix products, dot_f32(): lax.dot_general(lhs, rhs, (dims, ((), ())), preferred_element_type=jnp.fl...  31.3 us
    all_gather x1, waiting for transfers between devices, per_device(): small = jnp.sum(lax.all_gather(small, 'fsdp'), axis=0)  29.1 us
    reshape x1, local copies, waits for them, and re-layouts, per_device(): weight_lo = dense_weight[:STRIDE].reshape(half, row_width)  28.7 us
    reshape x1, local copies, waits for them, and re-layouts, per_device(): weight_hi = dense_weight[STRIDE:].reshape(half, row_width)  28.2 us
    slice x1, local copies, waits for them, and re-layouts, per_device(): weight_hi = dense_weight[STRIDE:].reshape(half, row_width)  25.8 us
  transfers between devices with their start and end apart: 8, of which 3 were waited for; matrix products, arithmetic and copies ran while one was open for 33% of the time, Pallas kernels for 0%

profile of v1, /device:TPU:32, one launch (start us, length us, event | category | flops | bytes accessed | tf_op | source)
XLA Modules:
  0.0 460.7 jit_solution(11023715925383192615)
XLA Ops:
  28.2 11.2 %broadcast_multiply_fusion = bf16[8,32,16,32,16]{4,3,2,1,0:T(8,128)(2,1)} fusion(bf16[32,32]{1,0:T(8,128)(2,1)S(1)} %fusion.39, bf16[8,32,16,16]{3,2,1,0:T(8,128)(2,1)S(1)} %copy.23), kind=kLoop, calls=%fused_computation.2 | loop fusion | flops 2097152 | bytes 4327424 | tf_op jit(solution)/shard_map/mul | solution.py:89
  39.4 25.8 %fusion.44 = (bf16[4,32,16,32,16]{4,3,2,1,0:T(8,128)(2,1)}, bf16[4,32,16,32,16]{4,3,2,1,0:T(8,128)(2,1)}) fusion(bf16[8,32,16,32,16]{4,3,2,1,0:T(8,128)(2,1)} %broadcast_multiply_fusion), kind=kLoop, calls=%fused_computation.87 | loop fusion | bytes 8388608 | tf_op jit(solution)/shard_map/slice | solution.py:93
  65.2 28.7 %reshape.249 = bf16[2048,512]{1,0:T(8,128)(2,1)} reshape(bf16[4,32,16,32,16]{4,3,2,1,0:T(8,128)(2,1)} %get-tuple-element.29) | data formatting | bytes 4194304 | tf_op jit(solution)/shard_map/reshape | solution.py:92
  93.9 28.2 %reshape.250 = bf16[2048,512]{1,0:T(8,128)(2,1)S(1)} reshape(bf16[4,32,16,32,16]{4,3,2,1,0:T(8,128)(2,1)} %get-tuple-element.28) | data formatting | bytes 4194304 | tf_op jit(solution)/shard_map/reshape | solution.py:93
  123.7 2.6 fusion.45
  127.0 2.2 copy.32
  134.2 4.5 fusion.15
  146.3 2.8 convolution_add_fusion.1
  149.1 19.8 %reshape.255 = f32[4,32,16,32,16]{4,3,2,1,0:T(8,128)} reshape(f32[2048,512]{1,0:T(8,128)} %convolution_add_fusion.1) | data formatting | bytes 8388608 | tf_op jit(solution)/shard_map/reshape | solution.py:120
  170.6 2.8 convolution_add_fusion
  173.4 19.8 %reshape.257 = f32[4,32,16,32,16]{4,3,2,1,0:T(8,128)} reshape(f32[2048,512]{1,0:T(8,128)} %convolution_add_fusion) | data formatting | bytes 8388608 | tf_op jit(solution)/shard_map/reshape | solution.py:120
  193.2 25.6 %multiply_reduce_fusion.1 = (f32[4,32,16,16]{3,2,1,0:T(8,128)S(1)}, f32[4,32,16,16]{3,2,1,0:T(8,128)}) fusion(f32[4,32,16,32,16]{4,3,2,1,0:T(8,128)} %reshape.255, f32[32,32]{1,0:T(8,128)S(1)} %fusion.38, f32[4,32,16,32,16]{4,3,2,1,0:T(8,128)} %reshape.257), kind=kLoop, calls=%fused_computation.1 | loop fusion | flops 4128768 | bytes 8654848 | tf_op jit(solution)/shard_map/reduce_sum | solution.py:122
  218.8 2.7 pad_maximum_fusion.1
  221.5 2.9 reshape.258
  230.4 4.2 pad_maximum_fusion
  239.8 5.8 %collective-permute-start.3 = (f32[4,512]{1,0:T(4,128)S(1)}, f32[4,512]{1,0:T(4,128)S(1)}, u32[]{:S(2)}, u32[]{:S(2)}) collective-permute-start(f32[4,512]{1,0:T(4,128)S(1)} %slice.92), channel_id=1, source_target_pairs={{0,16},{16,32},{32,48},{48,64},{64,80},{80,96},{96,112},{112,128},... | collective-permute-start | bytes 24584 | tf_op jit(solution)/shard_map/ppermute | solution.py:19
  245.6 3.7 fusion.46
  249.3 29.1 %all-gather.5.cloned.1.call-done = f32[16,129,512]{2,1,0:T(8,128)} async-done(((f32[1,129,512]{2,1,0:T(8,128)}), f32[16,129,512]{2,1,0:T(8,128)}) %all-gather.5.cloned.1.call-update) | async-done | bytes 4227088 | tf_op jit(solution)/shard_map/all_gather | solution.py:137
  278.3 2.8 reduce_sum.59
  281.1 65.7 %reduce-scatter.2.cloned.1.call-done = f32[256,512]{1,0:T(8,128)} async-done(((f32[4096,512]{1,0:T(8,128)}), f32[256,512]{1,0:T(8,128)}) %reduce-scatter.2.cloned.1.call-update) | async-done | bytes 524304 | tf_op jit(solution)/shard_map/reduce_scatter | solution.py:107
  348.9 4.3 fusion.1
  353.1 3.0 reshape.254
  358.1 4.1 fusion.16
  362.2 86.7 %all-reduce.2.cloned.1.call-done = f32[385,512]{1,0:T(8,128)} async-done(((f32[385,512]{1,0:T(8,128)}), f32[385,512]{1,0:T(8,128)}) %all-reduce.2.cloned.1.call-update) | async-done | bytes 788496 | tf_op jit(solution)/shard_map/psum | solution.py:138
  (140 shorter events, 56.0 us)
Async XLA Ops:
  7.2 10.6 %copy-start.5 = (bf16[1,1024,512]{2,1,0:T(8,128)(2,1)S(1)}, bf16[1,1024,512]{2,1,0:T(8,128)(2,1)}, u32[]{:S(2)}) copy-start(bf16[1,1024,512]{2,1,0:T(8,128)(2,1)} %param.9) | copy-start | bytes 3145732
  7.2 127.0 %all-gather.3.cloned.1.call-start = ((), (), s32[]{:S(2)}) async-start(), calls=%async_computation.1 | async-start | bytes 4456448 | tf_op jit(solution)/shard_map/all_gather | solution.py:97
  8.0 118.4 %collective-permute-start.1 = (s32[4]{0:T(128)S(1)}, s32[4]{0:T(128)S(1)}, u32[]{:S(2)}, u32[]{:S(2)}) collective-permute-start(s32[4]{0:T(128)S(1)} %slice_bitcast_fusion.2), channel_id=1, source_target_pairs={{16,0},{32,16},{48,32},{64,48},{80,64},{96,80},{112,96},{128,112},... | collective-permute-start | bytes 56 | tf_op jit(solution)/shard_map/ppermute | solution.py:19
  10.0 120.8 %collective-permute-start = (bf16[4,512]{1,0:T(4,128)(2,1)S(1)}, bf16[4,512]{1,0:T(4,128)(2,1)S(1)}, u32[]{:S(2)}, u32[]{:S(2)}) collective-permute-start(bf16[4,512]{1,0:T(4,128)(2,1)S(1)} %slice_bitcast_fusion.1), channel_id=1, source_target_pairs={{16,0},{32,16},{48,32},{64,48},{80,64},{96,80},{112,96},{128,112},... | collective-permute-start | bytes 12296 | tf_op jit(solution)/shard_map/ppermute | solution.py:19
  11.9 120.2 %collective-permute-start.2 = (bf16[4,512]{1,0:T(4,128)(2,1)S(1)}, bf16[4,512]{1,0:T(4,128)(2,1)S(1)}, u32[]{:S(2)}, u32[]{:S(2)}) collective-permute-start(bf16[4,512]{1,0:T(4,128)(2,1)S(1)} %slice_bitcast_fusion), channel_id=1, source_target_pairs={{16,0},{32,16},{48,32},{64,48},{80,64},{96,80},{112,96},{128,112},... | collective-permute-start | bytes 12296 | tf_op jit(solution)/shard_map/ppermute | solution.py:19
  13.3 265.1 %all-gather.5.cloned.1.call-start = ((), (), s32[]{:S(2)}) async-start(), calls=%async_computation.3 | async-start | bytes 4734976 | tf_op jit(solution)/shard_map/all_gather | solution.py:137
  17.8 2.8 copy-start.4
  22.1 3.6 copy-start.26
  93.9 28.2 %copy-start.14 = (bf16[1,1020,512]{2,1,0:T(8,128)(2,1)S(1)}, bf16[1,1020,512]{2,1,0:T(8,128)(2,1)}, u32[]{:S(2)}) copy-start(bf16[1,1020,512]{2,1,0:T(8,128)(2,1)} %slice.86) | copy-start | bytes 3133444
  130.8 3.1 copy-start.2
  133.2 6.5 %copy-start.21 = (bf16[256,512]{1,0:T(8,128)(2,1)}, bf16[256,512]{1,0:T(8,128)(2,1)S(1)}, u32[]{:S(2)}) copy-start(bf16[256,512]{1,0:T(8,128)(2,1)S(1)} %multiply_convert_fusion) | copy-start | bytes 786436
  134.2 4.5 copy-start.28
  138.7 2.0 copy-start
  138.7 2.6 copy-start.23
  141.3 1.8 copy-start.13
  144.4 1.9 copy-start.10
  221.5 6.3 %copy-start.18 = (bf16[256,2048]{1,0:T(8,128)(2,1)S(1)}, bf16[256,2048]{1,0:T(8,128)(2,1)}, u32[]{:S(2)}) copy-start(bf16[256,2048]{1,0:T(8,128)(2,1)} %copy-done.17) | copy-start | bytes 3145732
  227.8 119.1 %reduce-scatter.2.cloned.1.call-start = ((), (), s32[]{:S(2)}) async-start(), calls=%async_computation.2 | async-start | bytes 8912896 | tf_op jit(solution)/shard_map/reduce_scatter | solution.py:107
  227.8 1.8 copy-start.20
  234.6 214.2 %all-reduce.2.cloned.1.call-start = ((), (), s32[]{:S(2)}) async-start(), calls=%async_computation.4 | async-start | bytes 1605632 | tf_op jit(solution)/shard_map/psum | solution.py:138
  239.8 118.3 %collective-permute-start.3 = (f32[4,512]{1,0:T(4,128)S(1)}, f32[4,512]{1,0:T(4,128)S(1)}, u32[]{:S(2)}, u32[]{:S(2)}) collective-permute-start(f32[4,512]{1,0:T(4,128)S(1)} %slice.92), channel_id=1, source_target_pairs={{0,16},{16,32},{32,48},{48,64},{64,80},{80,96},{96,112},{112,128},... | collective-permute-start | bytes 24584 | tf_op jit(solution)/shard_map/ppermute | solution.py:19
  281.1 67.7 %copy-start.1 = (f32[32,8,4,512]{3,1,2,0:T(8,128)S(1)}, f32[32,8,4,512]{3,1,2,0:T(8,128)}, u32[]{:S(2)}) copy-start(f32[32,8,4,512]{3,1,2,0:T(8,128)} %copy.32) | copy-start | bytes 6291460
  353.1 3.0 copy-start.9
  356.2 1.9 copy-start.6
  (13 other events, 17.5 us)
Sparse Core Ops, SparseCore 0:
  13.4 50.0 all-gather.2
  227.9 50.4 all-gather.4
  280.9 65.9 reduce-scatter.1
  350.6 98.2 all-reduce.1
